TPU v7x, 512 devices: a whole 4x8x8 slice. The times are simulated.
512 devices in a mesh: dp: 32 (over x, z), mp: 16 (over y, core).
Axes of the slice: x: 4, y: 8, z: 8, core: 2. Of those that a mesh axis runs over, the one named last changes fastest.
Arguments:
- hidden_rows: bfloat16 [16384, 8192], P('dp', 'mp'), may hold values from -6 to 6
- base_weight: bfloat16 [8192, 4096], P('mp'), may hold values from -0.0625 to 0.0625
- adapter_down: bfloat16 [32, 64, 8192], P('dp', None, 'mp'), may hold values from -0.0625 to 0.0625
- adapter_up: bfloat16 [32, 64, 4096], P('dp', None, 'mp'), may hold values from -0.75 to 0.75
- adapter_of_row: int32 [16384, 1], P('dp'), may hold values from 0 to 31; in each aligned block of 512 rows (0 to 511, 512 to 1023, ...) at most 32 rows name the same one
- holder_map: int32 [32], replicated, may hold values from 0 to 31, each once
Outputs:
- projected: bfloat16 [16384, 4096], P('dp', 'mp')
Inputs may be any that keep to these rules, and one draw needn't show every extreme that they name: `adapter_of_row`: within the 512 rows of one index of dp (aligned blocks), no adapter is named by more than 32 rows; every adapter is named by some row. `holder_map`: each of the 32 slots holds exactly one adapter.
All inputs are finite; a program needn't handle non-finite values.
Results may differ from a plain program's by a relative error of at most 0.02.
Values may be sent and summed in bfloat16 or wider, within the bound.
No kernel may reach another device: no remote copies, remote signals or barrier semaphores. Data moves between devices by JAX's collectives and lax.ppermute only.
A program may use at most 64 MiB of HBM per device.

v0:
```python
import jax
import jax.numpy as jnp
from jax import lax
from jax.sharding import PartitionSpec as P


def per_device(hidden_rows, base_weight, adapter_down, adapter_up, adapter_of_row, holder_map):
    row_count, feat_width = hidden_rows.shape
    holders = lax.axis_size("dp")
    capacity = 2 * row_count // holders
    adapter_ids = adapter_of_row[:, 0]
    matches = adapter_ids[:, None] == jnp.arange(holder_map.shape[0], dtype=jnp.int32)[None, :]
    slot_of_row = jnp.sum(jnp.where(matches, holder_map[None, :], 0), axis=1)
    members = (slot_of_row[:, None] == jnp.arange(holders, dtype=jnp.int32)[None, :]).astype(
        jnp.int32
    )
    earlier = jnp.cumsum(members, axis=0) - members
    position = jnp.sum(earlier * members, axis=1)
    destination = slot_of_row * capacity + position
    packed = (
        jnp.zeros((holders * capacity, feat_width), jnp.bfloat16).at[destination].set(hidden_rows)
    )
    packed = packed.reshape(holders, capacity, feat_width)
    base_terms = jnp.dot(hidden_rows, base_weight, preferred_element_type=jnp.float32)
    base_total = lax.psum_scatter(
        base_terms.astype(jnp.bfloat16), "mp", scatter_dimension=1, tiled=True
    ).astype(jnp.float32)
    section = packed
    partial_value = jnp.einsum(
        "hcf,hkf->hck",
        section,
        lax.all_gather(adapter_down, "dp", axis=0, tiled=True),
        preferred_element_type=jnp.float32,
    )
    reduced = lax.psum(partial_value.astype(jnp.bfloat16), "mp")
    section = reduced
    buckets = jnp.einsum(
        "hck,hko->hco",
        section,
        lax.all_gather(adapter_up, "dp", axis=0, tiled=True),
        preferred_element_type=jnp.float32,
    ).astype(jnp.bfloat16)
    adapter_out = buckets.reshape(holders * capacity, buckets.shape[2])[destination]
    return (base_total + adapter_out.astype(jnp.float32)).astype(jnp.bfloat16)


def solution(mesh):
    placed = (
        P("dp", "mp"),
        P("mp", None),
        P("dp", None, "mp"),
        P("dp", None, "mp"),
        P("dp", None),
        P(),
    )
    return jax.shard_map(
        per_device, mesh=mesh, in_specs=placed, out_specs=P("dp", "mp"), check_vma=False
    )
```

profile of v0, /device:TPU:27, one launch (start us, length us, event | category | flops | bytes accessed | tf_op | source)
XLA Modules:
  0.0 372.1 jit_solution(2252982581453105532)
XLA Ops:
  6.5 0.0 copy-start
  6.5 0.0 all-gather.3.cloned.1.call-start
  6.5 0.7 all-gather.3.cloned.1.call-update
  7.3 0.0 all-gather.5.cloned.1.call-start
  7.3 0.7 all-gather.5.cloned.1.call-update
  8.0 0.0 all-reduce.2.cloned.1.call-start
  8.1 0.8 select_reduce_fusion
  8.9 1.2 reduce-window.6
  10.0 0.2 slice_reduce_fusion
  10.3 0.1 fusion.4
  10.4 3.2 scatter_custom_fusion
  13.6 80.2 %all-gather.3.cloned.1.call-done = bf16[32,64,512]{2,1,0:T(8,128)(2,1)} async-done(((bf16[1,64,512]{2,1,0:T(8,128)(2,1)}), bf16[32,64,512]{2,1,0:T(8,128)(2,1)}) %all-gather.3.cloned.1.call-update) | async-done | bytes 2097168 | tf_op jit(solution)/shard_map/all_gather | solution.py:32
  93.9 3.0 convolution_convert_fusion.2
  96.9 0.0 all-reduce.2.cloned.1.call-update
  96.9 0.0 reduce-scatter.2.cloned.1.call-start
  96.9 0.0 copy-done
  96.9 6.5 %convolution_convert_fusion = bf16[512,4096]{1,0:T(8,128)(2,1)} fusion(bf16[512,512]{1,0:T(8,128)(2,1)S(1)} %copy-done, bf16[512,4096]{1,0:T(8,128)(2,1)} %param.7), kind=kOutput, calls=%fused_computation.2 | convolution fusion | flops 2149580800 | bytes 8912896 | tf_op jit(solution)/shard_map/dot_general | solution.py:24
  103.5 0.0 reduce-scatter.2.cloned.1.call-update
  103.5 72.3 %all-gather.5.cloned.1.call-done = bf16[32,64,256]{2,1,0:T(8,128)(2,1)} async-done(((bf16[1,64,256]{2,1,0:T(8,128)(2,1)}), bf16[32,64,256]{2,1,0:T(8,128)(2,1)}) %all-gather.5.cloned.1.call-update) | async-done | bytes 1048592 | tf_op jit(solution)/shard_map/all_gather | solution.py:40
  175.8 119.3 %all-reduce.2.cloned.1.call-done = bf16[32,32,64]{2,1,0:T(8,128)(2,1)} async-done(((bf16[32,32,64]{2,1,0:T(8,128)(2,1)}), bf16[32,32,64]{2,1,0:T(8,128)(2,1)}) %all-reduce.2.cloned.1.call-update) | async-done | bytes 131088 | tf_op jit(solution)/shard_map/psum | solution.py:35
  295.1 1.6 convolution_convert_fusion.1
  296.7 2.0 gather_fusion
  298.7 65.1 %reduce-scatter.2.cloned.1.call-done = bf16[512,256]{1,0:T(8,128)(2,1)} async-done(((bf16[512,4096]{1,0:T(8,128)(2,1)}), bf16[512,256]{1,0:T(8,128)(2,1)}) %reduce-scatter.2.cloned.1.call-update) | async-done | bytes 262160 | tf_op jit(solution)/shard_map/reduce_scatter | solution.py:25
  363.8 1.7 add_convert_fusion
  (6 shorter events, 0.1 us)
Async XLA Ops:
  6.5 90.4 %copy-start = (bf16[512,512]{1,0:T(8,128)(2,1)S(1)}, bf16[512,512]{1,0:T(8,128)(2,1)}, u32[]{:S(2)}) copy-start(bf16[512,512]{1,0:T(8,128)(2,1)} %param.6) | copy-start | bytes 1572868
  6.5 87.3 %all-gather.3.cloned.1.call-start = ((), (), s32[]{:S(2)}) async-start(), calls=%async_computation.2 | async-start | bytes 2162688 | tf_op jit(solution)/shard_map/all_gather | solution.py:32
  7.3 168.6 %all-gather.5.cloned.1.call-start = ((), (), s32[]{:S(2)}) async-start(), calls=%async_computation.4 | async-start | bytes 1081344 | tf_op jit(solution)/shard_map/all_gather | solution.py:40
  8.0 287.1 %all-reduce.2.cloned.1.call-start = ((), (), s32[]{:S(2)}) async-start(), calls=%async_computation.3 | async-start | bytes 524288 | tf_op jit(solution)/shard_map/psum | solution.py:35
  96.9 266.9 %reduce-scatter.2.cloned.1.call-start = ((), (), s32[]{:S(2)}) async-start(), calls=%async_computation.1 | async-start | bytes 4456448 | tf_op jit(solution)/shard_map/reduce_scatter | solution.py:25
Sparse Core Ops, SparseCore 0:
  10.5 83.2 all-gather.2
  97.1 78.7 all-gather.4
  178.2 116.8 all-reduce.1
  298.0 65.7 reduce-scatter.1
where the time goes:
time: 372 us
  waiting for transfers between devices  338 us (91%)
  between operations  13.2 us (4%)
  matrix products  11.1 us (3%)
  local copies, waits for them, and re-layouts  5.4 us (1%)
  other arithmetic  3.85 us (1%)
    psum x1, waiting for transfers between devices, per_device(): reduced = lax.psum(partial_value.astype(jnp.bfloat16), 'mp')  119 us
    all_gather x1, waiting for transfers between devices, per_device(): lax.all_gather(adapter_down, 'dp', axis=0, tiled=True)  80.2 us
    all_gather x1, waiting for transfers between devices, per_device(): lax.all_gather(adapter_up, 'dp', axis=0, tiled=True)  72.3 us
    reduce_scatter x1, waiting for transfers between devices, per_device(): lax.psum_scatter(base_terms.astype(jnp.bfloat16), 'mp', scatter_dimension...  65.1 us
  transfers between devices with their start and end apart: 4, of which 4 were waited for; matrix products, arithmetic and copies ran while one was open for 5% of the time, Pallas kernels for 0%

commit v1 on v0

--- a/solution.py
+++ b/solution.py
@@ -29,7 +29,9 @@
     partial_value = jnp.einsum(
         "hcf,hkf->hck",
         section,
-        lax.all_gather(adapter_down, "dp", axis=0, tiled=True),
+        jnp.concatenate(
+            lax.all_to_all(jnp.stack([adapter_down] * lax.axis_size("dp")), "dp", 0, 0), axis=0
+        ),
         preferred_element_type=jnp.float32,
     )
     reduced = lax.psum(partial_value.astype(jnp.bfloat16), "mp")

time: 372 us -> 266 us (0.72)
  the two profiles are of different devices: /device:TPU:27 before, /device:TPU:2 now
where the time goes in v1:
time: 266 us
  waiting for transfers between devices  217 us (82%)
  between operations  14.9 us (6%)
  starting transfers between devices  13.6 us (5%)
  matrix products  9.63 us (4%)
  local copies, waits for them, and re-layouts  7.86 us (3%)
  other arithmetic  3.15 us (1%)
    psum x1, waiting for transfers between devices, per_device(): reduced = lax.psum(partial_value.astype(jnp.bfloat16), 'mp')  73.3 us
    reduce_scatter x1, waiting for transfers between devices, per_device(): lax.psum_scatter(base_terms.astype(jnp.bfloat16), 'mp', scatter_dimension...  65.6 us
    all_to_all x1, waiting for transfers between devices, per_device(): lax.all_to_all(jnp.stack([adapter_down] * lax.axis_size('dp')), 'dp', 0, 0)  42.9 us
    all_gather x1, waiting for transfers between devices, per_device(): lax.all_gather(adapter_up, 'dp', axis=0, tiled=True)  34.1 us
    all_to_all x1, starting transfers between devices, per_device(): lax.all_to_all(jnp.stack([adapter_down] * lax.axis_size('dp')), 'dp', 0, 0)  13.5 us
    dot_general x1, matrix products, per_device(): jnp.dot(hidden_rows, base_weight, preferred_element_type=jnp.float32)  6.63 us
  transfers between devices with their start and end apart: 4, of which 4 were waited for; matrix products, arithmetic and copies ran while one was open for 6% of the time, Pallas kernels for 0%

profile of v1, /device:TPU:2, one launch (start us, length us, event | category | flops | bytes accessed | tf_op | source)
XLA Modules:
  0.0 265.7 jit_solution(995550648300299792)
XLA Ops:
  7.4 0.0 copy-start
  7.4 0.0 copy-start.1
  7.4 2.5 stack.2
  9.8 13.5 %all-to-all-start = ((bf16[32,1,64,512]{3,2,1,0:T(8,128)(2,1)}), bf16[32,1,64,512]{3,2,1,0:T(8,128)(2,1)S(1)}, u32[]{:S(2)}, u32[]{:S(2)}) async-start(bf16[32,1,64,512]{3,2,1,0:T(8,128)(2,1)} %stack.2), calls=%async_computation.1 | async-start | bytes 4194304 | tf_op jit(solution)/shard_map/all_to_all | solution.py:33
  23.3 0.0 all-gather.2.cloned.1.call-start
  23.3 0.7 all-gather.2.cloned.1.call-update
  24.0 0.0 all-reduce.2.cloned.1.call-start
  24.1 0.0 copy-done
  24.1 0.0 copy-done.1
  24.1 0.1 select_reduce_fusion
  24.2 1.2 reduce-window.6
  25.4 0.2 slice_reduce_fusion
  25.6 0.1 fusion.9
  25.8 3.2 %scatter_custom_fusion = bf16[1024,512]{1,0:T(8,128)(2,1)S(1)} fusion(s32[512]{0:T(512)S(1)} %bitcast.40, bf16[512,512]{1,0:T(8,128)(2,1)} %param.6, bf16[]{:T(256)} %constant.4.clone.1), kind=kCustom, calls=%fused_computation.8 | custom fusion | bytes 1049088 | tf_op jit(solution)/shard_map/scatter | solution.py:21
  29.0 42.9 %all-to-all-done = bf16[32,1,64,512]{3,2,1,0:T(8,128)(2,1)S(1)} async-done(((bf16[32,1,64,512]{3,2,1,0:T(8,128)(2,1)}), bf16[32,1,64,512]{3,2,1,0:T(8,128)(2,1)S(1)}, u32[]{:S(2)}, u32[]{:S(2)}) %all-to-all-start) | async-done | bytes 2097184 | tf_op jit(solution)/shard_map/all_to_all | solution.py:33
  71.9 1.4 fusion.2
  73.3 0.0 all-reduce.2.cloned.1.call-update
  73.3 0.0 reduce-scatter.2.cloned.1.call-start
  73.4 6.6 %convolution_convert_fusion = bf16[512,4096]{1,0:T(8,128)(2,1)} fusion(bf16[512,512]{1,0:T(8,128)(2,1)} %param.6, bf16[512,4096]{1,0:T(8,128)(2,1)} %param.7), kind=kOutput, calls=%fused_computation.2 | convolution fusion | flops 2149580800 | bytes 8912896 | tf_op jit(solution)/shard_map/dot_general | solution.py:24
  80.0 0.0 reduce-scatter.2.cloned.1.call-update
  80.1 34.1 %all-gather.2.cloned.1.call-done = bf16[32,64,256]{2,1,0:T(8,128)(2,1)} async-done(((bf16[1,64,256]{2,1,0:T(8,128)(2,1)}), bf16[32,64,256]{2,1,0:T(8,128)(2,1)}) %all-gather.2.cloned.1.call-update) | async-done | bytes 1048592 | tf_op jit(solution)/shard_map/all_gather | solution.py:42
  114.1 73.3 %all-reduce.2.cloned.1.call-done = bf16[32,32,64]{2,1,0:T(8,128)(2,1)} async-done(((bf16[32,32,64]{2,1,0:T(8,128)(2,1)}), bf16[32,32,64]{2,1,0:T(8,128)(2,1)}) %all-reduce.2.cloned.1.call-update) | async-done | bytes 131088 | tf_op jit(solution)/shard_map/psum | solution.py:37
  187.4 1.6 convolution_convert_fusion.1
  189.0 2.0 gather_fusion
  191.0 65.6 %reduce-scatter.2.cloned.1.call-done = bf16[512,256]{1,0:T(8,128)(2,1)} async-done(((bf16[512,4096]{1,0:T(8,128)(2,1)}), bf16[512,256]{1,0:T(8,128)(2,1)}) %reduce-scatter.2.cloned.1.call-update) | async-done | bytes 262160 | tf_op jit(solution)/shard_map/reduce_scatter | solution.py:25
  256.6 1.7 add_convert_fusion
  (6 shorter events, 0.1 us)
Async XLA Ops:
  7.4 16.7 %copy-start = (s32[512,1]{0,1:T(1,128)S(1)}, s32[512,1]{0,1:T(1,128)}, u32[]{:S(2)}) copy-start(s32[512,1]{0,1:T(1,128)} %param.10) | copy-start | bytes 6148
  7.4 16.7 %copy-start.1 = (s32[32]{0:T(128)S(1)}, s32[32]{0:T(128)}, u32[]{:S(2)}) copy-start(s32[32]{0:T(128)} %param.11) | copy-start | bytes 388
  9.8 62.1 %all-to-all-start = ((bf16[32,1,64,512]{3,2,1,0:T(8,128)(2,1)}), bf16[32,1,64,512]{3,2,1,0:T(8,128)(2,1)S(1)}, u32[]{:S(2)}, u32[]{:S(2)}) async-start(bf16[32,1,64,512]{3,2,1,0:T(8,128)(2,1)} %stack.2), calls=%async_computation.1 | async-start | bytes 4194304 | tf_op jit(solution)/shard_map/all_to_all | solution.py:33
  23.3 90.8 %all-gather.2.cloned.1.call-start = ((), (), s32[]{:S(2)}) async-start(), calls=%async_computation.4 | async-start | bytes 1081344 | tf_op jit(solution)/shard_map/all_gather | solution.py:42
  24.0 163.4 %all-reduce.2.cloned.1.call-start = ((), (), s32[]{:S(2)}) async-start(), calls=%async_computation.3 | async-start | bytes 524288 | tf_op jit(solution)/shard_map/psum | solution.py:37
  73.3 183.2 %reduce-scatter.2.cloned.1.call-start = ((), (), s32[]{:S(2)}) async-start(), calls=%async_computation.2 | async-start | bytes 4456448 | tf_op jit(solution)/shard_map/reduce_scatter | solution.py:25
Sparse Core Ops, SparseCore 0:
  27.8 86.2 all-gather.1
Sparse Core Ops, SparseCore 1:
  73.4 113.9 all-reduce.1
  190.3 66.2 reduce-scatter.1

commit v2 on v0

--- a/solution.py
+++ b/solution.py
@@ -32,7 +32,7 @@
         lax.all_gather(adapter_down, "dp", axis=0, tiled=True),
         preferred_element_type=jnp.float32,
     )
-    reduced = lax.psum(partial_value.astype(jnp.bfloat16), "mp")
+    reduced = jnp.sum(lax.all_gather(partial_value.astype(jnp.bfloat16), "mp"), axis=0)
     section = reduced
     buckets = jnp.einsum(
         "hck,hko->hco",

time: 372 us -> 302 us (0.81)
  the two profiles are of different devices: /device:TPU:27 before, /device:TPU:31 now
where the time goes in v2:
time: 302 us
  waiting for transfers between devices  265 us (88%)
  between operations  13.2 us (4%)
  matrix products  11.1 us (4%)
  other arithmetic  6.92 us (2%)
  local copies, waits for them, and re-layouts  5.4 us (2%)
    all_gather x1, waiting for transfers between devices, per_device(): lax.all_gather(adapter_down, 'dp', axis=0, tiled=True)  80.3 us
    all_gather x1, waiting for transfers between devices, per_device(): lax.all_gather(adapter_up, 'dp', axis=0, tiled=True)  75.8 us
    reduce_scatter x1, waiting for transfers between devices, per_device(): lax.psum_scatter(base_terms.astype(jnp.bfloat16), 'mp', scatter_dimension...  67.9 us
    all_gather x1, waiting for transfers between devices, per_device(): lax.all_gather(partial_value.astype(jnp.bfloat16), 'mp')  39.7 us
    dot_general x1, matrix products, per_device(): jnp.dot(hidden_rows, base_weight, preferred_element_type=jnp.float32)  6.57 us
  transfers between devices with their start and end apart: 4, of which 4 were waited for; matrix products, arithmetic and copies ran while one was open for 6% of the time, Pallas kernels for 0%

profile of v2, /device:TPU:31, one launch (start us, length us, event | category | flops | bytes accessed | tf_op | source)
XLA Modules:
  0.0 301.7 jit_solution(7433611121004292582)
XLA Ops:
  6.5 0.0 copy-start
  6.5 0.0 all-gather.5.cloned.1.call-start
  6.5 0.7 all-gather.5.cloned.1.call-update
  7.3 0.0 all-gather.9.cloned.1.call-start
  7.3 0.8 select_reduce_fusion
  8.1 1.2 reduce-window.6
  9.3 0.2 slice_reduce_fusion
  9.5 0.1 fusion.4
  9.7 3.2 %scatter_custom_fusion = bf16[1024,512]{1,0:T(8,128)(2,1)S(1)} fusion(s32[512]{0:T(512)S(1)} %bitcast.36, bf16[512,512]{1,0:T(8,128)(2,1)} %param.6, bf16[]{:T(256)} %constant.4.clone.1), kind=kCustom, calls=%fused_computation.6 | custom fusion | bytes 1049088 | tf_op jit(solution)/shard_map/scatter | solution.py:21
  12.9 80.3 %all-gather.5.cloned.1.call-done = bf16[32,64,512]{2,1,0:T(8,128)(2,1)} async-done(((bf16[1,64,512]{2,1,0:T(8,128)(2,1)}), bf16[32,64,512]{2,1,0:T(8,128)(2,1)}) %all-gather.5.cloned.1.call-update) | async-done | bytes 2097168 | tf_op jit(solution)/shard_map/all_gather | solution.py:32
  93.2 3.0 convolution_convert_fusion.2
  96.2 0.0 all-gather.9.cloned.1.call-update
  96.2 0.0 all-gather.7.cloned.1.call-start
  96.2 0.7 all-gather.7.cloned.1.call-update
  96.9 0.0 reduce-scatter.2.cloned.1.call-start
  97.0 0.0 copy-done
  97.0 6.6 %convolution_convert_fusion = bf16[512,4096]{1,0:T(8,128)(2,1)} fusion(bf16[512,512]{1,0:T(8,128)(2,1)S(1)} %copy-done, bf16[512,4096]{1,0:T(8,128)(2,1)} %param.7), kind=kOutput, calls=%fused_computation.2 | convolution fusion | flops 2149580800 | bytes 8912896 | tf_op jit(solution)/shard_map/dot_general | solution.py:24
  103.6 0.0 reduce-scatter.2.cloned.1.call-update
  103.6 39.7 %all-gather.9.cloned.1.call-done = bf16[512,32,64]{2,1,0:T(8,128)(2,1)} async-done(((bf16[32,32,64]{2,1,0:T(8,128)(2,1)}), bf16[512,32,64]{2,1,0:T(8,128)(2,1)}) %all-gather.9.cloned.1.call-update) | async-done | bytes 2097168 | tf_op jit(solution)/shard_map/all_gather | solution.py:35
  143.3 3.1 %reduce_sum.32 = bf16[32,32,64]{2,1,0:T(8,128)(2,1)S(1)} reduce(bf16[16,32,32,64]{3,2,1,0:T(8,128)(2,1)} %bitcast.33, bf16[]{:T(256)} %constant.4.clone.1), dimensions={0}, to_apply=%region_6.7 | reduce | flops 983040 | bytes 2228226 | tf_op jit(solution)/shard_map/reduce_sum | solution.py:35
  146.4 75.8 %all-gather.7.cloned.1.call-done = bf16[32,64,256]{2,1,0:T(8,128)(2,1)} async-done(((bf16[1,64,256]{2,1,0:T(8,128)(2,1)}), bf16[32,64,256]{2,1,0:T(8,128)(2,1)}) %all-gather.7.cloned.1.call-update) | async-done | bytes 1048592 | tf_op jit(solution)/shard_map/all_gather | solution.py:40
  222.1 1.5 convolution_convert_fusion.1
  223.6 2.0 gather_fusion
  225.6 67.9 %reduce-scatter.2.cloned.1.call-done = bf16[512,256]{1,0:T(8,128)(2,1)} async-done(((bf16[512,4096]{1,0:T(8,128)(2,1)}), bf16[512,256]{1,0:T(8,128)(2,1)}) %reduce-scatter.2.cloned.1.call-update) | async-done | bytes 262160 | tf_op jit(solution)/shard_map/reduce_scatter | solution.py:25
  293.5 1.7 add_convert_fusion
  (6 shorter events, 0.1 us)
Async XLA Ops:
  6.5 90.4 %copy-start = (bf16[512,512]{1,0:T(8,128)(2,1)S(1)}, bf16[512,512]{1,0:T(8,128)(2,1)}, u32[]{:S(2)}) copy-start(bf16[512,512]{1,0:T(8,128)(2,1)} %param.6) | copy-start | bytes 1572868
  6.5 86.7 %all-gather.5.cloned.1.call-start = ((), (), s32[]{:S(2)}) async-start(), calls=%async_computation.2 | async-start | bytes 2162688 | tf_op jit(solution)/shard_map/all_gather | solution.py:32
  7.3 136.0 %all-gather.9.cloned.1.call-start = ((), (), s32[]{:S(2)}) async-start(), calls=%async_computation.4 | async-start | bytes 4456448 | tf_op jit(solution)/shard_map/all_gather | solution.py:35
  96.2 125.9 %all-gather.7.cloned.1.call-start = ((), (), s32[]{:S(2)}) async-start(), calls=%async_computation.3 | async-start | bytes 1081344 | tf_op jit(solution)/shard_map/all_gather | solution.py:40
  96.9 196.5 %reduce-scatter.2.cloned.1.call-start = ((), (), s32[]{:S(2)}) async-start(), calls=%async_computation.1 | async-start | bytes 4456448 | tf_op jit(solution)/shard_map/reduce_scatter | solution.py:25
Sparse Core Ops, SparseCore 0:
  10.5 82.6 all-gather.4
  96.3 46.9 all-gather.8
  146.5 75.5 all-gather.6
  224.8 68.6 reduce-scatter.1
